TPU v7x, 256 devices: a whole 4x4x8 slice. The times are simulated.
256 devices in a mesh: rep: 32 (over x, y, core), tp: 8 (over z).
Axes of the slice: x: 4, y: 4, z: 8, core: 2. Of those that a mesh axis runs over, the one named last changes fastest.
Arguments:
- prompt_rows: bfloat16 [20480, 2048], P(('rep', 'tp')), may hold values from -6 to 6
- prompt_pieces: int32 [32, 640], P('rep'), may hold values from 0 to 9, never falling along the last dimension, each value on 1 to 320 neighbouring positions
- decode_rows: bfloat16 [1280, 2048], P('rep'), may hold values from -6 to 6
- request_ages: int32 [1280], P('rep'), may hold values from 2 to 127
- migrate_to: int32 [512, 1], P('rep'), may hold values from 0 to 31, as said below
- past_cache: bfloat16 [1280, 2, 128, 2048], P('rep', None, None, 'tp'), may hold values from -8 to 8
- norm_gain: float32 [2048], replicated, may hold values from 0.5 to 1.5
- norm_bias: float32 [2048], replicated, may hold values from -2 to 2
- qkv_weight: bfloat16 [3, 2048, 2048], P(None, None, 'tp'), may hold values from -0.125 to 0.125
- qkv_bias: float32 [3, 2048], P(None, 'tp'), may hold values from -4 to 4
- out_weight: bfloat16 [2048, 2048], P('tp'), may hold values from -0.125 to 0.125
- out_bias: float32 [2048], replicated, may hold values from -3 to 3
Outputs:
- prompt_out: bfloat16 [20480, 2048], P(('rep', 'tp'))
- prompt_cache: bfloat16 [2, 20480, 2048], P(None, 'rep', 'tp')
- kept_out: bfloat16 [768, 2048], P('rep')
- kept_cache: bfloat16 [768, 2, 128, 2048], P('rep', None, None, 'tp')
- moved_out: bfloat16 [1024, 2048], P('rep')
- moved_cache: bfloat16 [1024, 2, 128, 2048], P('rep', None, None, 'tp')
Inputs may be any that keep to these rules, and one draw needn't show every extreme that they name: `migrate_to`: the 16 requests that leave one replica name 16 different target replicas, and one target replica is named by every replica. `prompt_pieces`: piece numbers never fall along a replica's prompt tokens; a piece has at most 320 tokens, and some piece exactly that many.
All inputs are finite; a program needn't handle non-finite values.
Results may differ from a plain program's by a relative error of at most 0.014.
Values may be sent and summed in bfloat16 or wider, within the bound.
No kernel may reach another device: no remote copies, remote signals or barrier semaphores. Data moves between devices by JAX's collectives and lax.ppermute only.
A program may use at most 128 MiB of HBM per device.

v0:
```python
import jax
import jax.numpy as jnp
from jax import lax
from jax.sharding import PartitionSpec as P

HEAD_DIM = 128
CAP = 1
EPSILON = 1e-05


def layer_norm(values, norm_gain, norm_bias):
    wide = values.astype(jnp.float32)
    center = jnp.mean(wide, axis=-1, keepdims=True)
    spread = jnp.mean(jnp.square(wide - center), axis=-1, keepdims=True)
    scaled = (wide - center) * lax.rsqrt(spread + EPSILON)
    return (scaled * norm_gain + norm_bias).astype(jnp.bfloat16)


def decode_partial(
    rows, cache, live, position, norm_gain, norm_bias, qkv_weight, qkv_bias, out_weight
):
    count = rows.shape[0]
    width = qkv_weight.shape[2]
    heads_here = width // HEAD_DIM
    length = cache.shape[2]
    normed = layer_norm(rows, norm_gain, norm_bias)
    projected = jnp.einsum("rd,cde->cre", normed, qkv_weight, preferred_element_type=jnp.float32)
    queries = (projected[0] + qkv_bias[0]).astype(jnp.bfloat16).reshape(count, heads_here, HEAD_DIM)
    key_new = (projected[1] + qkv_bias[1]).astype(jnp.bfloat16)
    value_new = (projected[2] + qkv_bias[2]).astype(jnp.bfloat16)
    old_keys = cache[:, 0].reshape(count, length, heads_here, HEAD_DIM)
    old_values = cache[:, 1].reshape(count, length, heads_here, HEAD_DIM)
    scale = HEAD_DIM ** (-0.5)
    scores = (
        jnp.einsum("rhe,rlhe->rhl", queries, old_keys, preferred_element_type=jnp.float32) * scale
    )
    own = (
        jnp.sum(
            queries.astype(jnp.float32)
            * key_new.astype(jnp.float32).reshape(count, heads_here, HEAD_DIM),
            axis=-1,
        )
        * scale
    )
    scores = jnp.where(live[:, None, :], scores, -1e30)
    highest = jnp.maximum(jnp.max(scores, axis=-1), own)
    weights = jnp.exp(scores - highest[..., None])
    own_weight = jnp.exp(own - highest)
    total = jnp.sum(weights, axis=-1) + own_weight
    probs = (weights / total[..., None]).astype(jnp.bfloat16)
    own_prob = (own_weight / total).astype(jnp.bfloat16)
    context = jnp.einsum("rhl,rlhe->rhe", probs, old_values, preferred_element_type=jnp.float32)
    context = context + own_prob.astype(jnp.float32)[..., None] * value_new.astype(
        jnp.float32
    ).reshape(count, heads_here, HEAD_DIM)
    context = context.reshape(count, width).astype(jnp.bfloat16)
    partial_value = jnp.dot(context, out_weight, preferred_element_type=jnp.float32)
    written = (jnp.arange(length)[None, :] == position[:, None])[:, :, None]
    new_keys = jnp.where(written, key_new[:, None, :], cache[:, 0])
    new_values = jnp.where(written, value_new[:, None, :], cache[:, 1])
    return (partial_value, jnp.stack([new_keys, new_values], axis=1))


def on_device(
    prompt_rows,
    prompt_pieces,
    decode_rows,
    request_ages,
    migrate_to,
    past_cache,
    norm_gain,
    norm_bias,
    qkv_weight,
    qkv_bias,
    out_weight,
    out_bias,
):
    rep_count = lax.axis_size("rep")
    width = qkv_weight.shape[2]
    heads_here = width // HEAD_DIM
    length = past_cache.shape[2]
    leaving = migrate_to.shape[0]
    staying = decode_rows.shape[0] - leaving
    slot_count = rep_count * CAP
    normed = layer_norm(lax.all_gather(prompt_rows, "tp", axis=0, tiled=True), norm_gain, norm_bias)
    projected = jnp.einsum("rd,cde->cre", normed, qkv_weight, preferred_element_type=jnp.float32)
    total_rows = projected.shape[1]
    queries = (projected[0] + qkv_bias[0]).astype(jnp.bfloat16)
    key_rows = (projected[1] + qkv_bias[1]).astype(jnp.bfloat16)
    value_rows = (projected[2] + qkv_bias[2]).astype(jnp.bfloat16)
    head_q = queries.reshape(total_rows, heads_here, HEAD_DIM)
    head_k = key_rows.reshape(total_rows, heads_here, HEAD_DIM)
    head_v = value_rows.reshape(total_rows, heads_here, HEAD_DIM)
    scores = jnp.einsum(
        "qhe,khe->hqk", head_q, head_k, preferred_element_type=jnp.float32
    ) * HEAD_DIM ** (-0.5)
    pieces = prompt_pieces[0]
    position = jnp.arange(total_rows)
    allowed = (pieces[:, None] == pieces[None, :]) & (position[None, :] <= position[:, None])
    scores = jnp.where(allowed[None], scores, -1e30)
    highest = jnp.max(scores, axis=-1, keepdims=True)
    weights = jnp.exp(scores - highest)
    probs = (weights / jnp.sum(weights, axis=-1, keepdims=True)).astype(jnp.bfloat16)
    context = jnp.einsum("hqk,khe->qhe", probs, head_v, preferred_element_type=jnp.float32)
    context = context.reshape(total_rows, width).astype(jnp.bfloat16)
    attended = lax.psum_scatter(
        jnp.dot(context, out_weight, preferred_element_type=jnp.float32).astype(jnp.bfloat16),
        "tp",
        scatter_dimension=0,
        tiled=True,
    ).astype(jnp.float32)
    prompt_out = (prompt_rows.astype(jnp.float32) + attended + out_bias).astype(jnp.bfloat16)
    prompt_cache = jnp.stack([key_rows, value_rows])
    targets = migrate_to[:, 0]
    onehot = (targets[:, None] == jnp.arange(rep_count)[None, :]).astype(jnp.float32)
    lower = (jnp.arange(leaving)[:, None] > jnp.arange(leaving)[None, :]).astype(jnp.float32)
    earlier = jnp.dot(lower, onehot)
    rank = jnp.sum(earlier * onehot, axis=1).astype(jnp.int32)
    slot = targets * CAP + rank
    placing = (jnp.arange(slot_count)[:, None] == slot[None, :]).astype(jnp.bfloat16)
    cells = jnp.arange(length)
    live = cells[None, :] < request_ages[:, None]
    partial_value, updated = decode_partial(
        decode_rows,
        past_cache,
        live,
        request_ages,
        norm_gain,
        norm_bias,
        qkv_weight,
        qkv_bias,
        out_weight,
    )
    summed = lax.psum(partial_value.astype(jnp.bfloat16), "tp").astype(jnp.float32)
    decode_out = (decode_rows.astype(jnp.float32) + summed + out_bias).astype(jnp.bfloat16)
    kept_out = decode_out[:staying]
    kept_cache = updated[:staying]
    send_cache = jnp.einsum(
        "so,oklh->sklh", placing, updated[staying:], preferred_element_type=jnp.float32
    ).astype(jnp.bfloat16)
    send_rows = jnp.dot(placing, decode_out[staying:], preferred_element_type=jnp.float32).astype(
        jnp.bfloat16
    )
    moved_cache, moved_out = (
        lax.all_to_all(send_cache, "rep", split_axis=0, concat_axis=0, tiled=True),
        lax.all_to_all(send_rows, "rep", split_axis=0, concat_axis=0, tiled=True),
    )
    return (prompt_out, prompt_cache, kept_out, kept_cache, moved_out, moved_cache)


def solution(mesh):
    placed = (
        P(("rep", "tp"), None),
        P("rep", None),
        P("rep", None),
        P("rep"),
        P("rep", None),
        P("rep", None, None, "tp"),
        P(),
        P(),
        P(None, None, "tp"),
        P(None, "tp"),
        P("tp", None),
        P(),
    )
    return jax.shard_map(
        on_device,
        mesh=mesh,
        in_specs=placed,
        out_specs=(
            P(("rep", "tp"), None),
            P(None, "rep", "tp"),
            P("rep", None),
            P("rep", None, None, "tp"),
            P("rep", None),
            P("rep", None, None, "tp"),
        ),
        check_vma=False,
    )
```

profile of v0, /device:TPU:8, one launch (start us, length us, event | category | flops | bytes accessed | tf_op | source)
XLA Modules:
  0.0 225.0 jit_solution(8399299144730349695)
XLA Ops:
  8.0 0.8 iota_compare_fusion.1
  8.9 1.0 convert_reduce_fusion.1
  10.0 1.1 fusion.32
  11.1 1.6 convolution_bitcast_fusion
  13.1 5.5 %fusion.71 = (bf16[40,1,128,256]{3,2,1,0:T(8,128)(2,1)}, bf16[40,1,128,256]{3,2,1,0:T(8,128)(2,1)}) fusion(bf16[40,2,128,256]{3,2,1,0:T(8,128)(2,1)} %param.17), kind=kLoop, calls=%fused_computation.117 | loop fusion | bytes 10485760 | tf_op jit(solution)/shard_map/slice | solution.py:31
  18.6 4.4 %copy.84 = bf16[40,1,128,256]{2,3,0,1:T(8,128)(2,1)} copy(bf16[40,1,128,256]{3,2,1,0:T(8,128)(2,1)} %get-tuple-element.36) | data formatting | bytes 5242880 | tf_op jit(solution)/shard_map/reshape;squeeze | solution.py:31
  23.0 2.6 %fusion.53 = f32[40,2,1,128]{3,2,1,0:T(1,128)S(1)} fusion(bf16[40,128,2,128]{1,3,2,0:T(8,128)(2,1)} %bitcast.75, bf16[40,2,128,1]{2,1,0,3:T(2,128)(2,1)S(1)} %get-tuple-element.49), kind=kOutput, calls=%fused_computation.82 | convolution fusion | flops 2621440 | bytes 2682880 | tf_op jit(solution)/shard_map/rhe,rlhe->rhl/dot_general | solution.py:35
  26.1 4.9 %reshape.266 = bf16[40,128,2,128]{3,2,1,0:T(2,128)(2,1)} reshape(bf16[40,1,128,256]{3,2,1,0:T(8,128)(2,1)} %get-tuple-element.37) | data formatting | bytes 5242880 | tf_op jit(solution)/shard_map/reshape;squeeze | solution.py:32
  31.1 4.4 %fusion.11 = f32[40,2,1,128]{3,2,1,0:T(1,128)S(1)} fusion(bf16[40,2,128,1]{2,0,1,3:T(8,128)(2,1)S(1)} %fusion.59, bf16[40,128,2,128]{3,2,1,0:T(2,128)(2,1)} %reshape.266), kind=kOutput, calls=%fused_computation.20 | convolution fusion | flops 2621440 | bytes 2682880 | tf_op jit(solution)/shard_map/rhl,rlhe->rhe/dot_general | solution.py:52
  35.7 1.0 convolution_convert_fusion.2
  37.2 1.0 fusion.23
  38.3 8.5 %broadcast_select_fusion = (bf16[40,1,128,256]{3,0,2,1:T(8,128)(2,1)}, bf16[40,1,128,256]{3,0,2,1:T(8,128)(2,1)}) fusion(pred[40,128]{0,1:T(8,128)(4,1)S(1)} %get-tuple-element.57, bf16[40,256]{1,0:T(8,128)(2,1)S(1)} %get-tuple-element.43, bf16[40,1,128,256]{3,2,1,0:T(8,128)(2,1)} %get-tuple-element.37, bf16[40,1,128,256]{3,2,1,0:T(8,128)(2,1)} %get-tuple-element.36, ...), kind=kLoop, calls=%fused_computation.26 | loop fusion | flops 2621440 | bytes 10531840 | tf_op jit(solution)/shard_map/jit(_where)/select_n | solution.py:60
  46.8 8.3 %all-gather.2.cloned.1.call-done = bf16[640,2048]{1,0:T(8,128)(2,1)} async-done(((bf16[80,2048]{1,0:T(8,128)(2,1)}), bf16[640,2048]{1,0:T(8,128)(2,1)}) %all-gather.2.cloned.1.call-update) | async-done | bytes 2621456 | tf_op jit(solution)/shard_map/all_gather | solution.py:85
  55.1 2.3 %convert_reduce_fusion = f32[640]{0:T(1024)S(1)} fusion(bf16[640,2048]{1,0:T(8,128)(2,1)} %all-gather.2.cloned.1.call-done), kind=kLoop, calls=%fused_computation.2 | loop fusion | flops 2620800 | bytes 2624000 | tf_op jit(solution)/shard_map/reduce_sum | solution.py:13
  57.6 0.8 fusion.3
  58.4 3.1 %fusion.25 = f32[3,640,256]{1,2,0:T(8,128)S(1)} fusion(bf16[3,2048,256]{2,1,0:T(8,128)(2,1)S(1)} %copy-done, bf16[640,2048]{1,0:T(8,128)(2,1)S(1)} %copy-done.3, f32[2048]{0:T(1024)S(1)} %copy-done.12, f32[2048]{0:T(1024)S(1)} %copy-done.13, f32[640]{0:T(1024)S(1)} %add_rsqrt_fusion, f32[640]{0:T(1024)S(1)} %broadcast_multiply_fusion), kind=kOutput, calls=%fused_computation.39 | convolution fusion | flops 2021130240 | bytes 7754752 | tf_op jit(solution)/shard_map/rd,cde->cre/dot_general | solution.py:86
  63.2 2.0 fusion.74
  66.4 2.4 %convolution_convert_fusion = bf16[640,2048]{1,0:T(8,128)(2,1)} fusion(bf16[640,256]{0,1:T(8,128)(2,1)S(1)} %bitcast.78, bf16[256,2048]{1,0:T(8,128)(2,1)S(1)} %copy-done.5), kind=kOutput, calls=%fused_computation.14 | convolution fusion | flops 672399360 | bytes 3997696 | tf_op jit(solution)/shard_map/dot_general | solution.py:107
  68.9 60.0 %all-reduce.2.cloned.1.call-done = bf16[40,2048]{1,0:T(8,128)(2,1)} async-done(((bf16[40,2048]{1,0:T(8,128)(2,1)}), bf16[40,2048]{1,0:T(8,128)(2,1)}) %all-reduce.2.cloned.1.call-update) | async-done | bytes 163856 | tf_op jit(solution)/shard_map/psum | solution.py:134
  128.8 1.0 fusion.37
  131.3 1.3 reduce.1
  132.6 1.6 reshape.267
  134.3 7.4 %all-to-all-start = ((bf16[32,2,1024]{2,1,0:T(2,128)(2,1)}), bf16[32,2,1024]{2,1,0:T(2,128)(2,1)S(1)}, u32[]{:S(2)}, u32[]{:S(2)}) async-start(bf16[32,2,1024]{2,1,0:T(2,128)(2,1)} %reshape.267), calls=%async_computation.1 | async-start | bytes 262144 | tf_op jit(solution)/shard_map/all_to_all | solution.py:146
  141.7 2.6 %convolution_convert_fusion.1 = bf16[32,2,128,256]{3,0,2,1:T(8,128)(2,1)S(1)} fusion(bf16[40,1,128,256]{3,0,2,1:T(8,128)(2,1)S(1)} %copy-done.2, bf16[40,1,128,256]{3,0,2,1:T(8,128)(2,1)} %get-tuple-element.51, s32[16]{0:T(128)S(1)} %convert_add_fusion.1), kind=kOutput, calls=%fused_computation.16 | convolution fusion | flops 73400832 | bytes 9437248 | tf_op jit(solution)/shard_map/so,oklh->sklh/dot_general | solution.py:138
  144.3 4.4 %copy.72 = bf16[32,2,128,256]{3,2,1,0:T(8,128)(2,1)} copy(bf16[32,2,128,256]{3,0,2,1:T(8,128)(2,1)S(1)} %convolution_convert_fusion.1) | data formatting | bytes 8388608 | tf_op jit(solution)/shard_map/convert_element_type | solution.py:140
  148.7 7.4 %all-to-all-start.1 = ((bf16[32,2,128,256]{3,2,1,0:T(8,128)(2,1)}), bf16[32,2,128,256]{3,2,1,0:T(8,128)(2,1)}, u32[]{:S(2)}, u32[]{:S(2)}) async-start(bf16[32,2,128,256]{3,2,1,0:T(8,128)(2,1)} %copy.72), calls=%async_computation.2 | async-start | bytes 8388608 | tf_op jit(solution)/shard_map/all_to_all | solution.py:145
  156.2 1.6 fusion.7
  157.8 2.4 %copy.74 = bf16[24,2,128,256]{3,2,1,0:T(8,128)(2,1)} copy(bf16[24,2,128,256]{3,0,2,1:T(8,128)(2,1)S(1)} %fusion.7) | data formatting | bytes 6291456
  161.6 49.1 %all-to-all-done.1 = bf16[32,2,128,256]{3,2,1,0:T(8,128)(2,1)} async-done(((bf16[32,2,128,256]{3,2,1,0:T(8,128)(2,1)}), bf16[32,2,128,256]{3,2,1,0:T(8,128)(2,1)}, u32[]{:S(2)}, u32[]{:S(2)}) %all-to-all-start.1) | async-done | bytes 4194336 | tf_op jit(solution)/shard_map/all_to_all | solution.py:145
  210.8 1.1 copy.73
  211.9 1.8 add_convert_fusion.2
  213.7 4.8 %copy.120 = bf16[32,2,128,256]{3,2,1,0:T(8,128)(2,1)} copy(bf16[32,2,128,256]{3,2,1,0:T(8,128)(2,1)} %all-to-all-done.1) | data formatting | bytes 8388608
  (76 shorter events, 8.5 us)
Async XLA Ops:
  7.2 4.0 %copy-start = (bf16[3,2048,256]{2,1,0:T(8,128)(2,1)S(1)}, bf16[3,2048,256]{2,1,0:T(8,128)(2,1)}, u32[]{:S(2)}) copy-start(bf16[3,2048,256]{2,1,0:T(8,128)(2,1)} %param.20) | copy-start | bytes 9437188
  7.2 5.7 %copy-start.15 = (f32[3,256]{1,0:T(4,128)S(1)}, f32[3,256]{1,0:T(4,128)}, u32[]{:S(2)}) copy-start(f32[3,256]{1,0:T(4,128)} %param.21) | copy-start | bytes 9220
  7.2 47.9 %all-gather.2.cloned.1.call-start = ((), (), s32[]{:S(2)}) async-start(), calls=%async_computation.3 | async-start | bytes 2949120 | tf_op jit(solution)/shard_map/all_gather | solution.py:85
  7.9 120.9 %all-reduce.2.cloned.1.call-start = ((), (), s32[]{:S(2)}) async-start(), calls=%async_computation.5 | async-start | bytes 327680 | tf_op jit(solution)/shard_map/psum | solution.py:134
  31.1 4.6 %copy-start.4 = (bf16[256,2048]{1,0:T(8,128)(2,1)S(1)}, bf16[256,2048]{1,0:T(8,128)(2,1)}, u32[]{:S(2)}) copy-start(bf16[256,2048]{1,0:T(8,128)(2,1)} %param.22) | copy-start | bytes 3145732
  31.1 5.8 %copy-start.16 = (s32[16,1]{0,1:T(1,128)S(1)}, s32[16,1]{0,1:T(1,128)}, u32[]{:S(2)}) copy-start(s32[16,1]{0,1:T(1,128)} %param.16) | copy-start | bytes 196
  31.1 6.1 %copy-start.14 = (s32[1,640]{1,0:T(1,128)S(1)}, s32[1,640]{1,0:T(1,128)}, u32[]{:S(2)}) copy-start(s32[1,640]{1,0:T(1,128)} %param.13) | copy-start | bytes 7684
  36.6 175.2 %reduce-scatter.2.cloned.1.call-start = ((), (), s32[]{:S(2)}) async-start(), calls=%async_computation.4 | async-start | bytes 2949120 | tf_op jit(solution)/shard_map/reduce_scatter | solution.py:106
  46.8 11.7 %copy-start.12 = (f32[2048]{0:T(1024)S(1)}, f32[2048]{0:T(1024)}, u32[]{:S(2)}) copy-start(f32[2048]{0:T(1024)} %param.19) | copy-start | bytes 24580
  55.1 2.5 %copy-start.3 = (bf16[640,2048]{1,0:T(8,128)(2,1)S(1)}, bf16[640,2048]{1,0:T(8,128)(2,1)}, u32[]{:S(2)}) copy-start(bf16[640,2048]{1,0:T(8,128)(2,1)} %all-gather.2.cloned.1.call-done) | copy-start | bytes 7864324
  55.1 3.4 %copy-start.13 = (f32[2048]{0:T(1024)S(1)}, f32[2048]{0:T(1024)}, u32[]{:S(2)}) copy-start(f32[2048]{0:T(1024)} %param.18) | copy-start | bytes 24580
  62.2 1.0 copy-start.10
  65.2 1.2 copy-start.5
  66.4 62.4 %copy-start.6 = (bf16[40,2048]{1,0:T(8,128)(2,1)S(1)}, bf16[40,2048]{1,0:T(8,128)(2,1)}, u32[]{:S(2)}) copy-start(bf16[40,2048]{1,0:T(8,128)(2,1)} %param.14) | copy-start | bytes 491524
  66.4 62.4 %copy-start.11 = (f32[2048]{0:T(1024)S(1)}, f32[2048]{0:T(1024)}, u32[]{:S(2)}) copy-start(f32[2048]{0:T(1024)} %param.23) | copy-start | bytes 24580
  68.8 72.9 %copy-start.2 = (bf16[40,1,128,256]{3,0,2,1:T(8,128)(2,1)S(1)}, bf16[40,1,128,256]{3,0,2,1:T(8,128)(2,1)}, u32[]{:S(2)}) copy-start(bf16[40,1,128,256]{3,0,2,1:T(8,128)(2,1)} %get-tuple-element.50) | copy-start | bytes 7864324
  129.8 0.7 copy-start.8
  134.3 14.5 %all-to-all-start = ((bf16[32,2,1024]{2,1,0:T(2,128)(2,1)}), bf16[32,2,1024]{2,1,0:T(2,128)(2,1)S(1)}, u32[]{:S(2)}, u32[]{:S(2)}) async-start(bf16[32,2,1024]{2,1,0:T(2,128)(2,1)} %reshape.267), calls=%async_computation.1 | async-start | bytes 262144 | tf_op jit(solution)/shard_map/all_to_all | solution.py:146
  148.7 62.0 %all-to-all-start.1 = ((bf16[32,2,128,256]{3,2,1,0:T(8,128)(2,1)}), bf16[32,2,128,256]{3,2,1,0:T(8,128)(2,1)}, u32[]{:S(2)}, u32[]{:S(2)}) async-start(bf16[32,2,128,256]{3,2,1,0:T(8,128)(2,1)} %copy.72), calls=%async_computation.2 | async-start | bytes 8388608 | tf_op jit(solution)/shard_map/all_to_all | solution.py:145
  157.8 2.4 %copy-start.9 = (bf16[40,2048]{1,0:T(8,128)(2,1)S(1)}, bf16[40,2048]{1,0:T(8,128)(2,1)}, u32[]{:S(2)}) copy-start(bf16[40,2048]{1,0:T(8,128)(2,1)} %copy-done.8) | copy-start | bytes 491524
  160.1 51.7 %copy-start.7 = (bf16[80,2048]{1,0:T(8,128)(2,1)S(1)}, bf16[80,2048]{1,0:T(8,128)(2,1)}, u32[]{:S(2)}) copy-start(bf16[80,2048]{1,0:T(8,128)(2,1)} %param.12) | copy-start | bytes 983044
  213.7 4.9 %copy-start.1 = (bf16[3,2048,256]{2,1,0:T(8,128)(2,1)S(1)}, bf16[3,2048,256]{2,1,0:T(8,128)(2,1)}, u32[]{:S(2)}) copy-start(bf16[3,2048,256]{2,1,0:T(8,128)(2,1)} %param.20) | copy-start | bytes 9437188
Sparse Core Ops, SparseCore 0:
  9.8 45.1 all-gather.1
  58.0 70.8 all-reduce.1
  131.6 42.1 reduce-scatter.1
where the time goes:
time: 226 us; the launch traced here: 225 us
  waiting for transfers between devices  118 us (52%)
  local copies, waits for them, and re-layouts  34.1 us (15%)
  other arithmetic  24.3 us (11%)
  matrix products  19.4 us (9%)
  starting transfers between devices  15.1 us (7%)
  between operations  14.1 us (6%)
    psum x1, waiting for transfers between devices, on_device(): lax.psum(partial_value.astype(jnp.bfloat16), 'tp').astype(jnp.float32)  60 us
    all_to_all x1, waiting for transfers between devices, on_device(): lax.all_to_all(send_cache, 'rep', split_axis=0, concat_axis=0, tiled=True)  49.1 us
    unnamed x40, local copies, waits for them, and re-layouts  12.8 us
    select_n x1, other arithmetic, decode_partial(): new_values = jnp.where(written, value_new[:, None, :], cache[:, 1])  8.49 us
    all_gather x1, waiting for transfers between devices, on_device(): lax.all_gather(prompt_rows, 'tp', axis=0, tiled=True)  8.31 us
    all_to_all x1, starting transfers between devices, on_device(): lax.all_to_all(send_cache, 'rep', split_axis=0, concat_axis=0, tiled=True)  7.44 us
    all_to_all x1, starting transfers between devices, on_device(): lax.all_to_all(send_rows, 'rep', split_axis=0, concat_axis=0, tiled=True)  7.41 us
    slice x1, local copies, waits for them, and re-layouts, decode_partial(): old_keys = cache[:, 0].reshape(count, length, heads_here, HEAD_DIM)  5.54 us
  transfers between devices with their start and end apart: 5, of which 3 were waited for; matrix products, arithmetic and copies ran while one was open for 31% of the time, Pallas kernels for 0%

commit v1 on v0

--- a/solution.py
+++ b/solution.py
@@ -6,6 +6,32 @@
 HEAD_DIM = 128
 CAP = 1
 EPSILON = 1e-05
+
+
+def return_all_the_plate(inp, axis_k):
+    device_axis = "tp"
+    even, x_next, after = (
+        lax.psum(1, axis_name=device_axis),
+        lax.axis_index(device_axis),
+        inp.shape[axis_k],
+    )
+    buffers = [(hop_no, (hop_no + 1) % even) for hop_no in range(even)]
+    copies = [(hop_no, (hop_no - 1) % even) for hop_no in range(even)]
+    plain = jnp.zeros((*inp.shape[:axis_k], even * after, *inp.shape[axis_k + 1 :]), inp.dtype)
+    plain = lax.dynamic_update_slice_in_dim(plain, inp, x_next * after, axis=axis_k)
+    carry = o_now = inp
+    part_now = even // 2
+    for c in tuple(range(1, part_now + 1)):
+        carry = lax.ppermute(carry, device_axis, buffers)
+        plain = lax.dynamic_update_slice_in_dim(
+            plain, carry, (x_next - c) % even * after, axis=axis_k
+        )
+        if c < even - part_now:
+            o_now = lax.ppermute(o_now, device_axis, copies)
+            plain = lax.dynamic_update_slice_in_dim(
+                plain, o_now, (x_next + c) % even * after, axis=axis_k
+            )
+    return plain
 
 
 def layer_norm(values, norm_gain, norm_bias):
@@ -82,7 +108,7 @@
     leaving = migrate_to.shape[0]
     staying = decode_rows.shape[0] - leaving
     slot_count = rep_count * CAP
-    normed = layer_norm(lax.all_gather(prompt_rows, "tp", axis=0, tiled=True), norm_gain, norm_bias)
+    normed = layer_norm(return_all_the_plate(prompt_rows, 0), norm_gain, norm_bias)
     projected = jnp.einsum("rd,cde->cre", normed, qkv_weight, preferred_element_type=jnp.float32)
     total_rows = projected.shape[1]
     queries = (projected[0] + qkv_bias[0]).astype(jnp.bfloat16)

time: 226 us -> 211 us (0.934)
  waiting for transfers between devices: 118 us -> 76.7 us
  starting transfers between devices: 15.1 us -> 27.7 us
  local copies, waits for them, and re-layouts: 34.1 us -> 44.4 us
    psum x1, waiting for transfers between devices: 60 us -> 10.1 us  [on_device(): lax.psum(partial_value.astype(jnp.bfloat16), 'tp').astype(jnp.float32)]
    ppermute x0 -> x7, waiting for transfers between devices: none -> 18.6 us  [the longest x4 14.6 us: return_all_the_plate(): carry = lax.ppermute(carry, device_axis, buffers)]
    ppermute x0 -> x7, starting transfers between devices: none -> 12.8 us  [the longest x3 12.8 us: return_all_the_plate(): o_now = lax.ppermute(o_now, device_axis, copies)]
    all_gather x1 -> x0, waiting for transfers between devices: 8.31 us -> none  [on_device(): lax.all_gather(prompt_rows, 'tp', axis=0, tiled=True)]
    dynamic_update_slice x0 -> x8, local copies, waits for them, and re-layouts: none -> 7.95 us  [the longest x4 3.99 us: return_all_the_plate(): lax.dynamic_update_slice_in_dim(plain, carry, (x_next - c) % even * after...]
    unnamed x40 -> x38, local copies, waits for them, and re-layouts: 12.8 us -> 12.6 us
  transfers between devices with their start and end apart: 5 -> 11, of which waited for: 3 -> 5; matrix products, arithmetic and copies ran while one was open for 31% -> 39% of each run, Pallas kernels for 0% -> 0%
where the time goes in v1:
time: 211 us; the launch traced here: 210 us
  waiting for transfers between devices  76.7 us (36%)
  local copies, waits for them, and re-layouts  44.4 us (21%)
  starting transfers between devices  27.7 us (13%)
  other arithmetic  25.7 us (12%)
  matrix products  20.9 us (10%)
  between operations  14.4 us (7%)
    all_to_all x1, waiting for transfers between devices, on_device(): lax.all_to_all(send_cache, 'rep', split_axis=0, concat_axis=0, tiled=True)  47.9 us
    ppermute x4, waiting for transfers between devices, return_all_the_plate(): carry = lax.ppermute(carry, device_axis, buffers)  14.6 us
    ppermute x3, starting transfers between devices, return_all_the_plate(): o_now = lax.ppermute(o_now, device_axis, copies)  12.8 us
    unnamed x38, local copies, waits for them, and re-layouts  12.6 us
    psum x1, waiting for transfers between devices, on_device(): lax.psum(partial_value.astype(jnp.bfloat16), 'tp').astype(jnp.float32)  10.1 us
    select_n x1, other arithmetic, decode_partial(): new_values = jnp.where(written, value_new[:, None, :], cache[:, 1])  8.44 us
    all_to_all x1, starting transfers between devices, on_device(): lax.all_to_all(send_cache, 'rep', split_axis=0, concat_axis=0, tiled=True)  7.44 us
    all_to_all x1, starting transfers between devices, on_device(): lax.all_to_all(send_rows, 'rep', split_axis=0, concat_axis=0, tiled=True)  7.41 us
  transfers between devices with their start and end apart: 11, of which 5 were waited for; matrix products, arithmetic and copies ran while one was open for 39% of the time, Pallas kernels for 0%

profile of v1, /device:TPU:8, one launch (start us, length us, event | category | flops | bytes accessed | tf_op | source)
XLA Modules:
  0.0 209.7 jit_solution(7403555252862364519)
XLA Ops:
  7.2 5.9 %collective-permute-start.1 = (bf16[80,2048]{1,0:T(8,128)(2,1)}, bf16[80,2048]{1,0:T(8,128)(2,1)}, u32[]{:S(2)}, u32[]{:S(2)}) collective-permute-start(bf16[80,2048]{1,0:T(8,128)(2,1)} %param.12), channel_id=1, source_target_pairs={{0,7},{1,0},{2,1},{3,2},{4,3},{5,4},{6,5},{7,6},{8,15},{9,8},{10,9... | collective-permute-start | bytes 983048 | tf_op jit(solution)/shard_map/ppermute | solution.py:30
  17.0 1.6 convolution_bitcast_fusion
  18.9 5.5 %fusion.71 = (bf16[40,1,128,256]{3,2,1,0:T(8,128)(2,1)}, bf16[40,1,128,256]{3,2,1,0:T(8,128)(2,1)}) fusion(bf16[40,2,128,256]{3,2,1,0:T(8,128)(2,1)} %param.17), kind=kLoop, calls=%fused_computation.125 | loop fusion | bytes 10485760 | tf_op jit(solution)/shard_map/slice | solution.py:57
  24.4 4.4 %copy.84 = bf16[40,1,128,256]{2,3,0,1:T(8,128)(2,1)} copy(bf16[40,1,128,256]{3,2,1,0:T(8,128)(2,1)} %get-tuple-element.36) | data formatting | bytes 5242880 | tf_op jit(solution)/shard_map/reshape;squeeze | solution.py:57
  28.8 2.5 %fusion.53 = f32[40,2,1,128]{3,2,1,0:T(1,128)S(1)} fusion(bf16[40,128,2,128]{1,3,2,0:T(8,128)(2,1)} %bitcast.75, bf16[40,2,128,1]{2,1,0,3:T(2,128)(2,1)S(1)} %get-tuple-element.49), kind=kOutput, calls=%fused_computation.82 | convolution fusion | flops 2621440 | bytes 2682880 | tf_op jit(solution)/shard_map/rhe,rlhe->rhl/dot_general | solution.py:61
  31.8 4.9 %reshape.266 = bf16[40,128,2,128]{3,2,1,0:T(2,128)(2,1)} reshape(bf16[40,1,128,256]{3,2,1,0:T(8,128)(2,1)} %get-tuple-element.37) | data formatting | bytes 5242880 | tf_op jit(solution)/shard_map/reshape;squeeze | solution.py:58
  36.7 4.4 %fusion.11 = f32[40,2,1,128]{3,2,1,0:T(1,128)S(1)} fusion(bf16[40,2,128,1]{2,0,1,3:T(8,128)(2,1)S(1)} %fusion.59, bf16[40,128,2,128]{3,2,1,0:T(2,128)(2,1)} %reshape.266), kind=kOutput, calls=%fused_computation.20 | convolution fusion | flops 2621440 | bytes 2682880 | tf_op jit(solution)/shard_map/rhl,rlhe->rhe/dot_general | solution.py:78
  42.3 8.4 %broadcast_select_fusion = (bf16[40,1,128,256]{3,0,2,1:T(8,128)(2,1)}, bf16[40,1,128,256]{3,0,2,1:T(8,128)(2,1)}) fusion(pred[40,128]{0,1:T(8,128)(4,1)S(1)} %get-tuple-element.57, bf16[40,256]{1,0:T(8,128)(2,1)S(1)} %get-tuple-element.43, bf16[40,1,128,256]{3,2,1,0:T(8,128)(2,1)} %get-tuple-element.37, bf16[40,1,128,256]{3,2,1,0:T(8,128)(2,1)} %get-tuple-element.36, ...), kind=kLoop, calls=%fused_computation.26 | loop fusion | flops 2621440 | bytes 10531840 | tf_op jit(solution)/shard_map/jit(_where)/select_n | solution.py:86
  50.7 1.8 broadcast_in_dim.44
  54.4 3.2 %collective-permute-start.3 = (bf16[80,2048]{1,0:T(8,128)(2,1)}, bf16[80,2048]{1,0:T(8,128)(2,1)S(1)}, u32[]{:S(2)}, u32[]{:S(2)}) collective-permute-start(bf16[80,2048]{1,0:T(8,128)(2,1)} %collective-permute-done.1), channel_id=1, source_target_pairs={{0,7},{1,0},{2,1},{3,2},{4,3},{5,4},{6,5},{7,6},{8,15},{9,8},{10,9... | collective-permute-start | bytes 983048 | tf_op jit(solution)/shard_map/ppermute | solution.py:30
  57.6 1.8 constant_dynamic-update-slice_fusion.6
  59.4 1.7 constant_dynamic-update-slice_fusion.5
  61.1 4.0 %collective-permute-done.3 = bf16[80,2048]{1,0:T(8,128)(2,1)S(1)} collective-permute-done((bf16[80,2048]{1,0:T(8,128)(2,1)}, bf16[80,2048]{1,0:T(8,128)(2,1)S(1)}, u32[]{:S(2)}, u32[]{:S(2)}) %collective-permute-start.3) | collective-permute-done | bytes 327712 | tf_op jit(solution)/shard_map/ppermute | solution.py:30
  65.2 3.6 %collective-permute-start.5 = (bf16[80,2048]{1,0:T(8,128)(2,1)S(1)}, bf16[80,2048]{1,0:T(8,128)(2,1)S(1)}, u32[]{:S(2)}, u32[]{:S(2)}) collective-permute-start(bf16[80,2048]{1,0:T(8,128)(2,1)S(1)} %collective-permute-done.3), channel_id=1, source_target_pairs={{0,7},{1,0},{2,1},{3,2},{4,3},{5,4},{6,5},{7,6},{8,15},{9,8},{10,9... | collective-permute-start | bytes 983048 | tf_op jit(solution)/shard_map/ppermute | solution.py:30
  70.2 7.8 %collective-permute-done.4 = bf16[80,2048]{1,0:T(8,128)(2,1)S(1)} collective-permute-done((bf16[80,2048]{1,0:T(8,128)(2,1)S(1)}, bf16[80,2048]{1,0:T(8,128)(2,1)S(1)}, u32[]{:S(2)}, u32[]{:S(2)}) %collective-permute-start.4) | collective-permute-done | bytes 327712 | tf_op jit(solution)/shard_map/ppermute | solution.py:25
  79.5 6.8 %collective-permute-done.6 = bf16[80,2048]{1,0:T(8,128)(2,1)S(1)} collective-permute-done((bf16[80,2048]{1,0:T(8,128)(2,1)S(1)}, bf16[80,2048]{1,0:T(8,128)(2,1)S(1)}, u32[]{:S(2)}, u32[]{:S(2)}) %collective-permute-start.6) | collective-permute-done | bytes 327712 | tf_op jit(solution)/shard_map/ppermute | solution.py:25
  87.1 2.2 %convert_reduce_fusion = f32[640]{0:T(1024)S(1)} fusion(bf16[640,2048]{1,0:T(8,128)(2,1)} %constant_dynamic-update-slice_fusion), kind=kLoop, calls=%fused_computation.2 | loop fusion | flops 2620800 | bytes 2624000 | tf_op jit(solution)/shard_map/reduce_sum | solution.py:39
  89.3 2.6 %fusion.3 = f32[640]{0:T(1024)S(1)} fusion(bf16[640,2048]{1,0:T(8,128)(2,1)} %constant_dynamic-update-slice_fusion, f32[640]{0:T(1024)S(1)} %broadcast_multiply_fusion), kind=kLoop, calls=%fused_computation.5 | loop fusion | flops 5242240 | bytes 2626560 | tf_op jit(solution)/shard_map/reduce_sum | solution.py:40
  91.9 4.7 %fusion.25 = f32[3,640,256]{1,2,0:T(8,128)S(1)} fusion(bf16[3,2048,256]{2,1,0:T(8,128)(2,1)S(1)} %copy-done, bf16[640,2048]{1,0:T(8,128)(2,1)} %constant_dynamic-update-slice_fusion, f32[2048]{0:T(1024)S(1)} %copy-done.12, f32[2048]{0:T(1024)S(1)} %copy-done.13, f32[640]{0:T(1024)S(1)} %add_rsqrt_fusion, f32[640]{0:T(1024)S(1)} %broadcast_multiply_fusion), kind=kOutput, calls=%fused_computation.39 | convolution fusion | flops 2021130240 | bytes 7754752 | tf_op jit(solution)/shard_map/rd,cde->cre/dot_general | solution.py:112
  98.3 2.0 fusion.74
  101.5 2.4 %convolution_convert_fusion = bf16[640,2048]{1,0:T(8,128)(2,1)} fusion(bf16[640,256]{0,1:T(8,128)(2,1)S(1)} %bitcast.78, bf16[256,2048]{1,0:T(8,128)(2,1)S(1)} %copy-done.4), kind=kOutput, calls=%fused_computation.14 | convolution fusion | flops 672399360 | bytes 3997696 | tf_op jit(solution)/shard_map/dot_general | solution.py:133
  104.2 10.1 %all-reduce.2.cloned.1.call-done = bf16[40,2048]{1,0:T(8,128)(2,1)} async-done(((bf16[40,2048]{1,0:T(8,128)(2,1)}), bf16[40,2048]{1,0:T(8,128)(2,1)}) %all-reduce.2.cloned.1.call-update) | async-done | bytes 163856 | tf_op jit(solution)/shard_map/psum | solution.py:160
  118.1 1.6 reshape.267
  119.8 7.4 %all-to-all-start = ((bf16[32,2,1024]{2,1,0:T(2,128)(2,1)}), bf16[32,2,1024]{2,1,0:T(2,128)(2,1)S(1)}, u32[]{:S(2)}, u32[]{:S(2)}) async-start(bf16[32,2,1024]{2,1,0:T(2,128)(2,1)} %reshape.267), calls=%async_computation.1 | async-start | bytes 262144 | tf_op jit(solution)/shard_map/all_to_all | solution.py:172
  127.2 2.6 %convolution_convert_fusion.1 = bf16[32,2,128,256]{3,0,2,1:T(8,128)(2,1)S(1)} fusion(bf16[40,1,128,256]{3,0,2,1:T(8,128)(2,1)S(1)} %copy-done.2, bf16[40,1,128,256]{3,0,2,1:T(8,128)(2,1)} %get-tuple-element.51, s32[16]{0:T(128)S(1)} %convert_add_fusion.1), kind=kOutput, calls=%fused_computation.16 | convolution fusion | flops 73400832 | bytes 9437248 | tf_op jit(solution)/shard_map/so,oklh->sklh/dot_general | solution.py:164
  129.8 4.4 %copy.72 = bf16[32,2,128,256]{3,2,1,0:T(8,128)(2,1)} copy(bf16[32,2,128,256]{3,0,2,1:T(8,128)(2,1)S(1)} %convolution_convert_fusion.1) | data formatting | bytes 8388608 | tf_op jit(solution)/shard_map/convert_element_type | solution.py:166
  134.2 7.4 %all-to-all-start.1 = ((bf16[32,2,128,256]{3,2,1,0:T(8,128)(2,1)}), bf16[32,2,128,256]{3,2,1,0:T(8,128)(2,1)}, u32[]{:S(2)}, u32[]{:S(2)}) async-start(bf16[32,2,128,256]{3,2,1,0:T(8,128)(2,1)} %copy.72), calls=%async_computation.2 | async-start | bytes 8388608 | tf_op jit(solution)/shard_map/all_to_all | solution.py:171
  141.7 1.6 fusion.7
  143.3 2.4 %copy.74 = bf16[24,2,128,256]{3,2,1,0:T(8,128)(2,1)} copy(bf16[24,2,128,256]{3,0,2,1:T(8,128)(2,1)S(1)} %fusion.7) | data formatting | bytes 6291456
  148.3 47.9 %all-to-all-done.1 = bf16[32,2,128,256]{3,2,1,0:T(8,128)(2,1)} async-done(((bf16[32,2,128,256]{3,2,1,0:T(8,128)(2,1)}), bf16[32,2,128,256]{3,2,1,0:T(8,128)(2,1)}, u32[]{:S(2)}, u32[]{:S(2)}) %all-to-all-start.1) | async-done | bytes 4194336 | tf_op jit(solution)/shard_map/all_to_all | solution.py:171
  196.2 1.8 add_convert_fusion.2
  198.0 4.8 %copy.128 = bf16[32,2,128,256]{3,2,1,0:T(8,128)(2,1)} copy(bf16[32,2,128,256]{3,2,1,0:T(8,128)(2,1)} %all-to-all-done.1) | data formatting | bytes 8388608
  (94 shorter events, 20.9 us)
Async XLA Ops:
  7.2 9.8 %copy-start = (bf16[3,2048,256]{2,1,0:T(8,128)(2,1)S(1)}, bf16[3,2048,256]{2,1,0:T(8,128)(2,1)}, u32[]{:S(2)}) copy-start(bf16[3,2048,256]{2,1,0:T(8,128)(2,1)} %param.20) | copy-start | bytes 9437188
  7.2 107.2 %all-reduce.2.cloned.1.call-start = ((), (), s32[]{:S(2)}) async-start(), calls=%async_computation.4 | async-start | bytes 327680 | tf_op jit(solution)/shard_map/psum | solution.py:160
  7.2 47.2 %collective-permute-start.1 = (bf16[80,2048]{1,0:T(8,128)(2,1)}, bf16[80,2048]{1,0:T(8,128)(2,1)}, u32[]{:S(2)}, u32[]{:S(2)}) collective-permute-start(bf16[80,2048]{1,0:T(8,128)(2,1)} %param.12), channel_id=1, source_target_pairs={{0,7},{1,0},{2,1},{3,2},{4,3},{5,4},{6,5},{7,6},{8,15},{9,8},{10,9... | collective-permute-start | bytes 983048 | tf_op jit(solution)/shard_map/ppermute | solution.py:30
  13.2 44.5 %collective-permute-start = (bf16[80,2048]{1,0:T(8,128)(2,1)}, bf16[80,2048]{1,0:T(8,128)(2,1)}, u32[]{:S(2)}, u32[]{:S(2)}) collective-permute-start(bf16[80,2048]{1,0:T(8,128)(2,1)} %param.12), channel_id=1, source_target_pairs={{0,1},{1,2},{2,3},{3,4},{4,5},{5,6},{6,7},{7,0},{8,9},{9,10},{10,1... | collective-permute-start | bytes 983048 | tf_op jit(solution)/shard_map/ppermute | solution.py:25
  36.7 4.5 %copy-start.3 = (bf16[256,2048]{1,0:T(8,128)(2,1)S(1)}, bf16[256,2048]{1,0:T(8,128)(2,1)}, u32[]{:S(2)}) copy-start(bf16[256,2048]{1,0:T(8,128)(2,1)} %param.22) | copy-start | bytes 3145732
  42.2 154.0 %reduce-scatter.2.cloned.1.call-start = ((), (), s32[]{:S(2)}) async-start(), calls=%async_computation.3 | async-start | bytes 2949120 | tf_op jit(solution)/shard_map/reduce_scatter | solution.py:132
  50.7 1.8 copy-start.6
  50.7 2.6 %copy-start.14 = (s32[1,640]{1,0:T(1,128)S(1)}, s32[1,640]{1,0:T(1,128)}, u32[]{:S(2)}) copy-start(s32[1,640]{1,0:T(1,128)} %param.13) | copy-start | bytes 7684
  54.4 10.7 %collective-permute-start.3 = (bf16[80,2048]{1,0:T(8,128)(2,1)}, bf16[80,2048]{1,0:T(8,128)(2,1)S(1)}, u32[]{:S(2)}, u32[]{:S(2)}) collective-permute-start(bf16[80,2048]{1,0:T(8,128)(2,1)} %collective-permute-done.1), channel_id=1, source_target_pairs={{0,7},{1,0},{2,1},{3,2},{4,3},{5,4},{6,5},{7,6},{8,15},{9,8},{10,9... | collective-permute-start | bytes 983048 | tf_op jit(solution)/shard_map/ppermute | solution.py:30
  57.6 11.1 %collective-permute-start.2 = (bf16[80,2048]{1,0:T(8,128)(2,1)}, bf16[80,2048]{1,0:T(8,128)(2,1)S(1)}, u32[]{:S(2)}, u32[]{:S(2)}) collective-permute-start(bf16[80,2048]{1,0:T(8,128)(2,1)} %collective-permute-done), channel_id=1, source_target_pairs={{0,1},{1,2},{2,3},{3,4},{4,5},{5,6},{6,7},{7,0},{8,9},{9,10},{10,1... | collective-permute-start | bytes 983048 | tf_op jit(solution)/shard_map/ppermute | solution.py:25
  65.2 13.6 %collective-permute-start.5 = (bf16[80,2048]{1,0:T(8,128)(2,1)S(1)}, bf16[80,2048]{1,0:T(8,128)(2,1)S(1)}, u32[]{:S(2)}, u32[]{:S(2)}) collective-permute-start(bf16[80,2048]{1,0:T(8,128)(2,1)S(1)} %collective-permute-done.3), channel_id=1, source_target_pairs={{0,7},{1,0},{2,1},{3,2},{4,3},{5,4},{6,5},{7,6},{8,15},{9,8},{10,9... | collective-permute-start | bytes 983048 | tf_op jit(solution)/shard_map/ppermute | solution.py:30
  68.7 9.3 %collective-permute-start.4 = (bf16[80,2048]{1,0:T(8,128)(2,1)S(1)}, bf16[80,2048]{1,0:T(8,128)(2,1)S(1)}, u32[]{:S(2)}, u32[]{:S(2)}) collective-permute-start(bf16[80,2048]{1,0:T(8,128)(2,1)S(1)} %collective-permute-done.2), channel_id=1, source_target_pairs={{0,1},{1,2},{2,3},{3,4},{4,5},{5,6},{6,7},{7,0},{8,9},{9,10},{10,1... | collective-permute-start | bytes 983048 | tf_op jit(solution)/shard_map/ppermute | solution.py:25
  78.0 8.3 %collective-permute-start.6 = (bf16[80,2048]{1,0:T(8,128)(2,1)S(1)}, bf16[80,2048]{1,0:T(8,128)(2,1)S(1)}, u32[]{:S(2)}, u32[]{:S(2)}) collective-permute-start(bf16[80,2048]{1,0:T(8,128)(2,1)S(1)} %collective-permute-done.4), channel_id=1, source_target_pairs={{0,1},{1,2},{2,3},{3,4},{4,5},{5,6},{6,7},{7,0},{8,9},{9,10},{10,1... | collective-permute-start | bytes 983048 | tf_op jit(solution)/shard_map/ppermute | solution.py:25
  87.1 4.8 %copy-start.12 = (f32[2048]{0:T(1024)S(1)}, f32[2048]{0:T(1024)}, u32[]{:S(2)}) copy-start(f32[2048]{0:T(1024)} %param.19) | copy-start | bytes 24580
  87.1 4.8 %copy-start.13 = (f32[2048]{0:T(1024)S(1)}, f32[2048]{0:T(1024)}, u32[]{:S(2)}) copy-start(f32[2048]{0:T(1024)} %param.18) | copy-start | bytes 24580
  97.3 1.0 copy-start.10
  100.3 1.2 copy-start.4
  101.5 2.4 %copy-start.15 = (s32[16,1]{0,1:T(1,128)S(1)}, s32[16,1]{0,1:T(1,128)}, u32[]{:S(2)}) copy-start(s32[16,1]{0,1:T(1,128)} %param.16) | copy-start | bytes 196
  101.5 12.9 %copy-start.5 = (bf16[40,2048]{1,0:T(8,128)(2,1)S(1)}, bf16[40,2048]{1,0:T(8,128)(2,1)}, u32[]{:S(2)}) copy-start(bf16[40,2048]{1,0:T(8,128)(2,1)} %param.14) | copy-start | bytes 491524
  103.9 10.4 %copy-start.11 = (f32[2048]{0:T(1024)S(1)}, f32[2048]{0:T(1024)}, u32[]{:S(2)}) copy-start(f32[2048]{0:T(1024)} %param.23) | copy-start | bytes 24580
  103.9 23.3 %copy-start.2 = (bf16[40,1,128,256]{3,0,2,1:T(8,128)(2,1)S(1)}, bf16[40,1,128,256]{3,0,2,1:T(8,128)(2,1)}, u32[]{:S(2)}) copy-start(bf16[40,1,128,256]{3,0,2,1:T(8,128)(2,1)} %get-tuple-element.50) | copy-start | bytes 7864324
  115.3 0.7 copy-start.8
  119.8 14.5 %all-to-all-start = ((bf16[32,2,1024]{2,1,0:T(2,128)(2,1)}), bf16[32,2,1024]{2,1,0:T(2,128)(2,1)S(1)}, u32[]{:S(2)}, u32[]{:S(2)}) async-start(bf16[32,2,1024]{2,1,0:T(2,128)(2,1)} %reshape.267), calls=%async_computation.1 | async-start | bytes 262144 | tf_op jit(solution)/shard_map/all_to_all | solution.py:172
  134.2 62.0 %all-to-all-start.1 = ((bf16[32,2,128,256]{3,2,1,0:T(8,128)(2,1)}), bf16[32,2,128,256]{3,2,1,0:T(8,128)(2,1)}, u32[]{:S(2)}, u32[]{:S(2)}) async-start(bf16[32,2,128,256]{3,2,1,0:T(8,128)(2,1)} %copy.72), calls=%async_computation.2 | async-start | bytes 8388608 | tf_op jit(solution)/shard_map/all_to_all | solution.py:171
  143.3 2.4 %copy-start.9 = (bf16[40,2048]{1,0:T(8,128)(2,1)S(1)}, bf16[40,2048]{1,0:T(8,128)(2,1)}, u32[]{:S(2)}) copy-start(bf16[40,2048]{1,0:T(8,128)(2,1)} %copy-done.8) | copy-start | bytes 491524
  145.6 50.6 %copy-start.7 = (bf16[80,2048]{1,0:T(8,128)(2,1)S(1)}, bf16[80,2048]{1,0:T(8,128)(2,1)}, u32[]{:S(2)}) copy-start(bf16[80,2048]{1,0:T(8,128)(2,1)} %param.12) | copy-start | bytes 983044
  198.0 4.9 %copy-start.1 = (bf16[3,2048,256]{2,1,0:T(8,128)(2,1)S(1)}, bf16[3,2048,256]{2,1,0:T(8,128)(2,1)}, u32[]{:S(2)}) copy-start(bf16[3,2048,256]{2,1,0:T(8,128)(2,1)} %param.20) | copy-start | bytes 9437188
Sparse Core Ops, SparseCore 0:
  42.4 71.9 all-reduce.1
  117.1 42.1 reduce-scatter.1
